TPU v7x, 128 devices: a whole 4x4x4 slice. The times are simulated.
128 devices in a mesh: dp: 16 (over z, y), vocab: 8 (over x, core).
Axes of the slice: x: 4, y: 4, z: 4, core: 2. Of those that a mesh axis runs over, the one named last changes fastest.
Arguments:
- hidden: bfloat16 [32, 512, 1024], P('dp'), may hold values from -24 to 24
- norm_gain: float32 [1024], replicated, may hold values from 0.5 to 1.5
- head: bfloat16 [1024, 32000], P('dp', 'vocab'), may hold values from -4 to 4
- targets: int32 [32, 512], P('dp'), may hold values from 0 to 31999
- lengths: int32 [32], P('dp'), may hold values from 1 to 512, 9216 in all
- groups: int32 [32, 1], P('dp'), may hold values from 0 to 3
- baseline: float32 [4], replicated, may hold values from -2 to 0
Outputs:
- logprob: float32 [32, 512], P('dp')
- entropy: float32 [32, 512], P('dp')
- group_shift: float32 [2, 4], replicated
Inputs may be any that keep to these rules, and one draw needn't show every extreme that they name: `groups`: every group holds at least one sequence.
All inputs are finite; a program needn't handle non-finite values. No bound on the sum of `lengths` on one device may be relied on, other than what follows from the above.
Results may differ from a plain program's by a relative error of at most 0.00045.
The roundings to bfloat16 on the way count: a program that leaves them out, or rounds other values in their place, can miss the bound.
Values may be sent and summed in bfloat16 or wider, within the bound.
No kernel may reach another device: no remote copies, remote signals or barrier semaphores. Data moves between devices by JAX's collectives and lax.ppermute only.
A program may use at most 64 MiB of HBM per device.

v0:
```python
import jax
import jax.numpy as jnp
from jax import lax
from jax.sharding import PartitionSpec as P


def per_device(hidden, norm_gain, head, targets, lengths, groups, baseline):
    seq_count, slot_count, width = hidden.shape
    total_rows = seq_count * slot_count
    block = min(512, total_rows)
    weights = lax.all_gather(head, "dp", axis=0, tiled=True)
    vocab_width = weights.shape[1]
    offset = lax.axis_index("vocab") * vocab_width
    flat = hidden.reshape(total_rows, width).astype(jnp.float32)
    square = jnp.mean(flat * flat, axis=-1, keepdims=True)
    normed = (flat * lax.rsqrt(square + 1e-05) * norm_gain[None, :]).astype(jnp.bfloat16)
    positions = jnp.arange(slot_count, dtype=jnp.int32)
    live = (positions[None, :] < lengths[:, None]).reshape(total_rows)
    wanted = targets.reshape(total_rows)
    column = jnp.arange(vocab_width, dtype=jnp.int32) + offset

    def local_stats(rows, picks):
        logits = jnp.dot(rows, weights, preferred_element_type=jnp.float32)
        local_top = jnp.max(logits, axis=-1)
        shifted = logits - local_top[:, None]
        expo = jnp.exp(shifted)
        local_total = jnp.sum(expo, axis=-1)
        local_spread = jnp.sum(expo * shifted, axis=-1)
        chosen = jnp.sum(jnp.where(column[None, :] == picks[:, None], logits, 0.0), axis=-1)
        return jnp.stack([local_top, local_total, local_spread, chosen], axis=0)

    parts = [
        local_stats(normed[start : start + block], wanted[start : start + block])
        for start in range(0, total_rows, block)
    ]
    stats = jnp.concatenate(parts, axis=1)
    vocab_count = lax.axis_size("vocab")
    spread_out = jnp.broadcast_to(stats[None], (vocab_count,) + stats.shape)
    gathered = lax.all_to_all(spread_out, "vocab", 0, 0, tiled=False)
    tops = gathered[:, 0]
    top = jnp.max(tops, axis=0)
    factor = jnp.exp(tops - top[None, :])
    total = jnp.sum(gathered[:, 1] * factor, axis=0)
    spread = jnp.sum(factor * (gathered[:, 2] + gathered[:, 1] * (tops - top[None, :])), axis=0)
    target = jnp.sum(gathered[:, 3], axis=0)
    log_total = jnp.log(total)
    logprob = target - top - log_total
    entropy = log_total - spread / total
    logprob = jnp.where(live, logprob, 0.0).reshape(seq_count, slot_count)
    entropy = jnp.where(live, entropy, 0.0).reshape(seq_count, slot_count)
    group_count = baseline.shape[0]
    member = (groups[:, 0][:, None] == jnp.arange(group_count, dtype=jnp.int32)[None, :]).astype(
        jnp.float32
    )
    seq_sums = jnp.stack(
        [jnp.sum(logprob, axis=1), jnp.sum(entropy, axis=1), lengths.astype(jnp.float32)], axis=1
    )
    partial_value = jnp.dot(member.T, seq_sums, precision=lax.Precision.HIGHEST)
    dp_count = lax.axis_size("dp")
    partial_out = jnp.broadcast_to(partial_value[None], (dp_count,) + partial_value.shape)
    group_value = jnp.sum(lax.all_to_all(partial_out, "dp", 0, 0, tiled=False), axis=0)
    group_lp, group_ent, group_cnt = (group_value[:, 0], group_value[:, 1], group_value[:, 2])
    shift = jnp.stack([group_lp / group_cnt - baseline, group_ent / group_cnt], axis=0)
    return (logprob, entropy, shift)


def solution(mesh):
    placed = (
        P("dp", None, None),
        P(),
        P("dp", "vocab"),
        P("dp", None),
        P("dp"),
        P("dp", None),
        P(),
    )
    return jax.shard_map(
        per_device,
        mesh=mesh,
        in_specs=placed,
        out_specs=(P("dp", None), P("dp", None), P()),
        check_vma=False,
    )
```

profile of v0, /device:TPU:0, one launch (start us, length us, event | category | flops | bytes accessed | tf_op | source)
XLA Modules:
  0.0 137.0 jit_solution(7105504285659255126)
XLA Ops:
  7.2 0.0 all-gather.2.cloned.1.call-start
  7.2 0.7 all-gather.2.cloned.1.call-update
  7.9 2.1 %multiply_reduce_fusion = f32[2,512]{1,0:T(2,128)S(1)} fusion(bf16[2,512,1024]{2,1,0:T(8,128)(2,1)} %param.7), kind=kLoop, calls=%fused_computation.11 | loop fusion | flops 3144704 | bytes 2101248 | tf_op jit(solution)/shard_map/reduce_sum | solution.py:15
  10.0 0.8 fusion.30
  10.8 2.1 %fusion.3 = bf16[1024,1024]{1,0:T(8,128)(2,1)S(1)} fusion(f32[1024]{0:T(1024)} %param.8, f32[1024]{0:T(1024)S(1)} %bitcast.54, bf16[2,512,1024]{2,1,0:T(8,128)(2,1)} %param.7), kind=kLoop, calls=%fused_computation.10 | loop fusion | flops 4194304 | bytes 4202496 | tf_op jit(solution)/shard_map/convert_element_type | solution.py:16
  12.9 70.6 %all-gather.2.cloned.1.call-done = bf16[1024,4000]{1,0:T(8,128)(2,1)} async-done(((bf16[64,4000]{1,0:T(8,128)(2,1)}), bf16[1024,4000]{1,0:T(8,128)(2,1)}) %all-gather.2.cloned.1.call-update) | async-done | bytes 8192016 | tf_op jit(solution)/shard_map/all_gather | solution.py:11
  83.6 7.2 %fusion.31 = (f32[512]{0:T(512)S(1)}, f32[512,4000]{0,1:T(8,128)S(1)}) fusion(bf16[1024,4000]{1,0:T(8,128)(2,1)} %all-gather.2.cloned.1.call-done, bf16[1024,1024]{1,0:T(8,128)(2,1)S(1)} %fusion.3), kind=kOutput, calls=%fused_computation.54 | convolution fusion | flops 4196351488 | bytes 17434624 | tf_op jit(solution)/shard_map/dot_general | solution.py:23
  90.8 7.2 %fusion.32 = (f32[512]{0:T(512)S(1)}, f32[512,4000]{0,1:T(8,128)S(1)}) fusion(bf16[1024,4000]{1,0:T(8,128)(2,1)} %all-gather.2.cloned.1.call-done, bf16[1024,1024]{1,0:T(8,128)(2,1)S(1)} %fusion.3), kind=kOutput, calls=%fused_computation.55 | convolution fusion | flops 4196351488 | bytes 17434624 | tf_op jit(solution)/shard_map/dot_general | solution.py:23
  97.9 0.0 copy-start
  98.0 0.0 copy-start.2
  98.0 0.0 copy-start.1
  98.0 6.6 %exponential_reduce_fusion.1 = (f32[512]{0:T(512)S(1)}, f32[512]{0:T(512)S(1)}, f32[512]{0:T(512)S(1)}, f32[512]{0:T(512)S(1)}, f32[512]{0:T(512)S(1)}, /*index=5*/f32[512]{0:T(512)S(1)}) fusion(f32[512,4000]{0,1:T(8,128)S(1)} %get-tuple-element.32, f32[512]{0:T(512)S(1)} %get-tuple-element.31, s32[512]{0:T(512)S(1)} %bitcast.63, s32[4000]{0:T(1024)S(1)} %iota_add_fusion, ...), kind=kLoop, calls=%fused_computation.3 | loop fusion | flops 28668928 | bytes 16420480 | tf_op jit(solution)/shard_map/reduce_sum | solution.py:27
  104.6 0.7 broadcast_in_dim.14
  105.2 4.3 %all-to-all-start = ((f32[8,4,1024]{2,1,0:T(4,128)}), f32[8,4,1024]{2,1,0:T(4,128)S(1)}, u32[]{:S(2)}, u32[]{:S(2)}) async-start(f32[8,4,1024]{2,1,0:T(4,128)} %broadcast_in_dim.14), calls=%async_computation | async-start | bytes 262144 | tf_op jit(solution)/shard_map/all_to_all | solution.py:39
  109.5 0.0 copy-done
  109.5 6.1 %all-to-all-done = f32[8,4,1024]{2,1,0:T(4,128)S(1)} async-done(((f32[8,4,1024]{2,1,0:T(4,128)}), f32[8,4,1024]{2,1,0:T(4,128)S(1)}, u32[]{:S(2)}, u32[]{:S(2)}) %all-to-all-start) | async-done | bytes 131104 | tf_op jit(solution)/shard_map/all_to_all | solution.py:39
  115.6 0.1 fusion.29
  115.8 0.8 fusion.27
  116.6 0.0 copy-done.2
  116.6 0.2 fusion.13
  116.8 12.7 %all_to_all.10 = f32[16,4,3]{1,2,0:T(4,128)S(1)} all-to-all(f32[16,4,3]{1,2,0:T(4,128)S(1)} %broadcast_in_dim.16), channel_id=1, replica_groups=mesh['dp'=16,'vocab'=8] {'dp'}, dimensions={0} | all-to-all | bytes 1536 | tf_op jit(solution)/shard_map/all_to_all | solution.py:61
  129.6 0.0 copy-done.1
  129.6 0.6 pad_maximum_fusion
  (13 shorter events, 0.2 us)
Async XLA Ops:
  7.2 76.4 %all-gather.2.cloned.1.call-start = ((), (), s32[]{:S(2)}) async-start(), calls=%async_computation.2 | async-start | bytes 8912896 | tf_op jit(solution)/shard_map/all_gather | solution.py:11
  97.9 11.6 %copy-start = (s32[2]{0:T(128)S(1)}, s32[2]{0:T(128)}, u32[]{:S(2)}) copy-start(s32[2]{0:T(128)} %param.11) | copy-start | bytes 28
  98.0 18.7 %copy-start.2 = (s32[2,1]{0,1:T(1,128)S(1)}, s32[2,1]{0,1:T(1,128)}, u32[]{:S(2)}) copy-start(s32[2,1]{0,1:T(1,128)} %param.12) | copy-start | bytes 28
  98.0 31.6 %copy-start.1 = (f32[4]{0:T(128)S(1)}, f32[4]{0:T(128)}, u32[]{:S(2)}) copy-start(f32[4]{0:T(128)} %param.13) | copy-start | bytes 52
  105.2 10.4 %all-to-all-start = ((f32[8,4,1024]{2,1,0:T(4,128)}), f32[8,4,1024]{2,1,0:T(4,128)S(1)}, u32[]{:S(2)}, u32[]{:S(2)}) async-start(f32[8,4,1024]{2,1,0:T(4,128)} %broadcast_in_dim.14), calls=%async_computation | async-start | bytes 262144 | tf_op jit(solution)/shard_map/all_to_all | solution.py:39
Sparse Core Ops, SparseCore 0:
  10.1 73.4 all-gather.1
where the time goes:
time: 137 us
  waiting for transfers between devices  77.4 us (56%)
  matrix products  14.5 us (11%)
  between operations  14.2 us (10%)
  blocking collectives  12.7 us (9%)
  other arithmetic  12.4 us (9%)
  starting transfers between devices  4.3 us (3%)
  local copies, waits for them, and re-layouts  1.47 us (1%)
    all_gather x1, waiting for transfers between devices, per_device(): weights = lax.all_gather(head, 'dp', axis=0, tiled=True)  70.6 us
    dot_general x2, matrix products, local_stats(): logits = jnp.dot(rows, weights, preferred_element_type=jnp.float32)  14.4 us
    all_to_all x1, blocking collectives, per_device(): lax.all_to_all(partial_out, 'dp', 0, 0, tiled=False)  12.7 us
    reduce_sum x1, other arithmetic, local_stats(): local_total = jnp.sum(expo, axis=-1)  6.58 us
    all_to_all x1, waiting for transfers between devices, per_device(): gathered = lax.all_to_all(spread_out, 'vocab', 0, 0, tiled=False)  6.09 us
    all_to_all x1, starting transfers between devices, per_device(): gathered = lax.all_to_all(spread_out, 'vocab', 0, 0, tiled=False)  4.26 us
  transfers between devices with their start and end apart: 2, of which 2 were waited for; matrix products, arithmetic and copies ran while one was open for 4% of the time, Pallas kernels for 0%

commit v1 on v0

--- a/solution.py
+++ b/solution.py
@@ -8,7 +8,28 @@
     seq_count, slot_count, width = hidden.shape
     total_rows = seq_count * slot_count
     block = min(512, total_rows)
-    weights = lax.all_gather(head, "dp", axis=0, tiled=True)
+    kept_arr, outcome_arr, b_now = (lax.axis_size("dp"), lax.axis_index("dp"), head.shape[0])
+    store = [kk * kept_arr if ix == 0 else kk for ix, kk in enumerate(head.shape)]
+    weights = lax.dynamic_update_slice_in_dim(
+        jnp.zeros(store, head.dtype), head, outcome_arr * b_now, axis=0
+    )
+    a_next = near = head
+    i = 1
+    while i < kept_arr // 2 + 1:
+        a_next = lax.ppermute(
+            a_next, axis_name="dp", perm=[(ix, (ix + 1) % kept_arr) for ix in range(kept_arr)]
+        )
+        weights = lax.dynamic_update_slice_in_dim(
+            weights, a_next, (outcome_arr - i) % kept_arr * b_now, axis=0
+        )
+        if 2 * i < kept_arr:
+            near = lax.ppermute(
+                near, axis_name="dp", perm=[(ix, (ix - 1) % kept_arr) for ix in range(kept_arr)]
+            )
+            weights = lax.dynamic_update_slice_in_dim(
+                weights, near, (outcome_arr + i) % kept_arr * b_now, axis=0
+            )
+        i = i + 1
     vocab_width = weights.shape[1]
     offset = lax.axis_index("vocab") * vocab_width
     flat = hidden.reshape(total_rows, width).astype(jnp.float32)

time: 137 us -> 164 us (1.20)
  starting transfers between devices: 4.3 us -> 43.1 us
  between operations: 14.2 us -> 1.17 us
  local copies, waits for them, and re-layouts: 1.47 us -> 4.18 us
  blocking collectives: 12.7 us -> 10.1 us
    ppermute x0 -> x15, waiting for transfers between devices: none -> 70.9 us  [the longest x8 70.9 us: per_device(): lax.ppermute(a_next, axis_name='dp', perm=[(ix, (ix + 1) % kept_arr) for...]
    all_gather x1 -> x0, waiting for transfers between devices: 70.6 us -> none  [per_device(): weights = lax.all_gather(head, 'dp', axis=0, tiled=True)]
    ppermute x0 -> x15, starting transfers between devices: none -> 38.8 us  [the longest x7 37.1 us: per_device(): lax.ppermute(near, axis_name='dp', perm=[(ix, (ix - 1) % kept_arr) for ix...]
    all_to_all x1, blocking collectives: 12.7 us -> 10.1 us  [per_device(): lax.all_to_all(partial_out, 'dp', 0, 0, tiled=False)]
    dynamic_update_slice x0 -> x16, local copies, waits for them, and re-layouts: none -> 1.67 us  [the longest x8 1.34 us: per_device(): lax.dynamic_update_slice_in_dim(weights, a_next, (outcome_arr - i) % kept...]
  transfers between devices with their start and end apart: 2 -> 16, of which waited for: 2 -> 9; matrix products, arithmetic and copies ran while one was open for 4% -> 5% of each run, Pallas kernels for 0% -> 0%
where the time goes in v1:
time: 164 us; the launch traced here: 163 us
  waiting for transfers between devices  77 us (47%)
  starting transfers between devices  43.1 us (26%)
  matrix products  13.8 us (8%)
  other arithmetic  13.6 us (8%)
  blocking collectives  10.1 us (6%)
  local copies, waits for them, and re-layouts  4.18 us (3%)
    ppermute x8, waiting for transfers between devices, per_device(): lax.ppermute(a_next, axis_name='dp', perm=[(ix, (ix + 1) % kept_arr) for...  70.9 us
    ppermute x7, starting transfers between devices, per_device(): lax.ppermute(near, axis_name='dp', perm=[(ix, (ix - 1) % kept_arr) for ix...  37.1 us
    dot_general x2, matrix products, local_stats(): logits = jnp.dot(rows, weights, preferred_element_type=jnp.float32)  13.7 us
    all_to_all x1, blocking collectives, per_device(): lax.all_to_all(partial_out, 'dp', 0, 0, tiled=False)  10.1 us
    reduce_sum x1, other arithmetic, local_stats(): local_total = jnp.sum(expo, axis=-1)  7.77 us
    all_to_all x1, waiting for transfers between devices, per_device(): gathered = lax.all_to_all(spread_out, 'vocab', 0, 0, tiled=False)  6.09 us
    all_to_all x1, starting transfers between devices, per_device(): gathered = lax.all_to_all(spread_out, 'vocab', 0, 0, tiled=False)  4.3 us
  transfers between devices with their start and end apart: 16, of which 9 were waited for; matrix products, arithmetic and copies ran while one was open for 5% of the time, Pallas kernels for 0%

profile of v1, /device:TPU:0, one launch (start us, length us, event | category | flops | bytes accessed | tf_op | source)
XLA Modules:
  0.0 163.1 jit_solution(17406810736019497409)
XLA Ops:
  0.6 0.0 copy-start
  0.6 1.8 %collective-permute-start = (bf16[64,4000]{1,0:T(8,128)(2,1)}, bf16[64,4000]{1,0:T(8,128)(2,1)}, u32[]{:S(2)}, u32[]{:S(2)}) collective-permute-start(bf16[64,4000]{1,0:T(8,128)(2,1)} %param.9), channel_id=1, source_target_pairs={{0,8},{8,16},{16,24},{24,32},{32,40},{40,48},{48,56},{56,64},{64,7... | collective-permute-start | bytes 1536008 | tf_op jit(solution)/shard_map/ppermute | solution.py:19
  2.4 5.0 %collective-permute-start.1 = (bf16[64,4000]{1,0:T(8,128)(2,1)}, bf16[64,4000]{1,0:T(8,128)(2,1)S(1)}, u32[]{:S(2)}, u32[]{:S(2)}) collective-permute-start(bf16[64,4000]{1,0:T(8,128)(2,1)} %param.9), channel_id=1, source_target_pairs={{0,120},{8,0},{16,8},{24,16},{32,24},{40,32},{48,40},{56,48},{64,5... | collective-permute-start | bytes 1536008 | tf_op jit(solution)/shard_map/ppermute | solution.py:26
  7.4 2.1 %multiply_reduce_fusion = f32[2,512]{1,0:T(2,128)S(1)} fusion(bf16[2,512,1024]{2,1,0:T(8,128)(2,1)} %param.7), kind=kLoop, calls=%fused_computation.11 | loop fusion | flops 3144704 | bytes 2101248 | tf_op jit(solution)/shard_map/reduce_sum | solution.py:36
  9.5 0.8 fusion.30
  10.3 2.1 %fusion.3 = bf16[1024,1024]{1,0:T(8,128)(2,1)S(1)} fusion(f32[1024]{0:T(1024)} %param.8, f32[1024]{0:T(1024)S(1)} %bitcast.54, bf16[2,512,1024]{2,1,0:T(8,128)(2,1)} %param.7), kind=kLoop, calls=%fused_computation.10 | loop fusion | flops 4194304 | bytes 4202496 | tf_op jit(solution)/shard_map/convert_element_type | solution.py:37
  12.7 1.0 broadcast_in_dim.15
  13.8 0.0 copy-done
  13.8 5.7 %collective-permute-done = bf16[64,4000]{1,0:T(8,128)(2,1)} collective-permute-done((bf16[64,4000]{1,0:T(8,128)(2,1)}, bf16[64,4000]{1,0:T(8,128)(2,1)}, u32[]{:S(2)}, u32[]{:S(2)}) %collective-permute-start) | collective-permute-done | bytes 512032 | tf_op jit(solution)/shard_map/ppermute | solution.py:19
  19.5 0.0 collective-permute-start.2
  19.6 0.0 collective-permute-done.1
  19.6 5.3 %collective-permute-start.3 = (bf16[64,4000]{1,0:T(8,128)(2,1)S(1)}, bf16[64,4000]{1,0:T(8,128)(2,1)S(1)}, u32[]{:S(2)}, u32[]{:S(2)}) collective-permute-start(bf16[64,4000]{1,0:T(8,128)(2,1)S(1)} %collective-permute-done.1), channel_id=1, source_target_pairs={{0,120},{8,0},{16,8},{24,16},{32,24},{40,32},{48,40},{56,48},{64,5... | collective-permute-start | bytes 1536008 | tf_op jit(solution)/shard_map/ppermute | solution.py:26
  24.9 1.1 constant_dynamic-update-slice_fusion.14
  26.0 10.1 %collective-permute-done.2 = bf16[64,4000]{1,0:T(8,128)(2,1)S(1)} collective-permute-done((bf16[64,4000]{1,0:T(8,128)(2,1)}, bf16[64,4000]{1,0:T(8,128)(2,1)S(1)}, u32[]{:S(2)}, u32[]{:S(2)}) %collective-permute-start.2) | collective-permute-done | bytes 512032 | tf_op jit(solution)/shard_map/ppermute | solution.py:19
  36.2 0.0 collective-permute-start.4
  36.2 0.0 collective-permute-done.3
  36.2 5.3 %collective-permute-start.5 = (bf16[64,4000]{1,0:T(8,128)(2,1)S(1)}, bf16[64,4000]{1,0:T(8,128)(2,1)S(1)}, u32[]{:S(2)}, u32[]{:S(2)}) collective-permute-start(bf16[64,4000]{1,0:T(8,128)(2,1)S(1)} %collective-permute-done.3), channel_id=1, source_target_pairs={{0,120},{8,0},{16,8},{24,16},{32,24},{40,32},{48,40},{56,48},{64,5... | collective-permute-start | bytes 1536008 | tf_op jit(solution)/shard_map/ppermute | solution.py:26
  41.6 10.1 %collective-permute-done.4 = bf16[64,4000]{1,0:T(8,128)(2,1)S(1)} collective-permute-done((bf16[64,4000]{1,0:T(8,128)(2,1)S(1)}, bf16[64,4000]{1,0:T(8,128)(2,1)S(1)}, u32[]{:S(2)}, u32[]{:S(2)}) %collective-permute-start.4) | collective-permute-done | bytes 512032 | tf_op jit(solution)/shard_map/ppermute | solution.py:19
  51.7 0.0 collective-permute-start.6
  51.7 0.0 collective-permute-done.5
  51.7 5.3 %collective-permute-start.7 = (bf16[64,4000]{1,0:T(8,128)(2,1)S(1)}, bf16[64,4000]{1,0:T(8,128)(2,1)S(1)}, u32[]{:S(2)}, u32[]{:S(2)}) collective-permute-start(bf16[64,4000]{1,0:T(8,128)(2,1)S(1)} %collective-permute-done.5), channel_id=1, source_target_pairs={{0,120},{8,0},{16,8},{24,16},{32,24},{40,32},{48,40},{56,48},{64,5... | collective-permute-start | bytes 1536008 | tf_op jit(solution)/shard_map/ppermute | solution.py:26
  57.2 9.3 %collective-permute-done.6 = bf16[64,4000]{1,0:T(8,128)(2,1)S(1)} collective-permute-done((bf16[64,4000]{1,0:T(8,128)(2,1)S(1)}, bf16[64,4000]{1,0:T(8,128)(2,1)S(1)}, u32[]{:S(2)}, u32[]{:S(2)}) %collective-permute-start.6) | collective-permute-done | bytes 512032 | tf_op jit(solution)/shard_map/ppermute | solution.py:19
  66.4 0.0 collective-permute-start.8
  66.4 0.0 collective-permute-done.7
  66.4 5.3 %collective-permute-start.9 = (bf16[64,4000]{1,0:T(8,128)(2,1)S(1)}, bf16[64,4000]{1,0:T(8,128)(2,1)S(1)}, u32[]{:S(2)}, u32[]{:S(2)}) collective-permute-start(bf16[64,4000]{1,0:T(8,128)(2,1)S(1)} %collective-permute-done.7), channel_id=1, source_target_pairs={{0,120},{8,0},{16,8},{24,16},{32,24},{40,32},{48,40},{56,48},{64,5... | collective-permute-start | bytes 1536008 | tf_op jit(solution)/shard_map/ppermute | solution.py:26
  71.9 8.4 %collective-permute-done.8 = bf16[64,4000]{1,0:T(8,128)(2,1)S(1)} collective-permute-done((bf16[64,4000]{1,0:T(8,128)(2,1)S(1)}, bf16[64,4000]{1,0:T(8,128)(2,1)S(1)}, u32[]{:S(2)}, u32[]{:S(2)}) %collective-permute-start.8) | collective-permute-done | bytes 512032 | tf_op jit(solution)/shard_map/ppermute | solution.py:19
  80.3 0.0 collective-permute-start.10
  80.3 0.0 collective-permute-done.9
  80.3 5.3 %collective-permute-start.11 = (bf16[64,4000]{1,0:T(8,128)(2,1)S(1)}, bf16[64,4000]{1,0:T(8,128)(2,1)S(1)}, u32[]{:S(2)}, u32[]{:S(2)}) collective-permute-start(bf16[64,4000]{1,0:T(8,128)(2,1)S(1)} %collective-permute-done.9), channel_id=1, source_target_pairs={{0,120},{8,0},{16,8},{24,16},{32,24},{40,32},{48,40},{56,48},{64,5... | collective-permute-start | bytes 1536008 | tf_op jit(solution)/shard_map/ppermute | solution.py:26
  85.7 7.5 %collective-permute-done.10 = bf16[64,4000]{1,0:T(8,128)(2,1)S(1)} collective-permute-done((bf16[64,4000]{1,0:T(8,128)(2,1)S(1)}, bf16[64,4000]{1,0:T(8,128)(2,1)S(1)}, u32[]{:S(2)}, u32[]{:S(2)}) %collective-permute-start.10) | collective-permute-done | bytes 512032 | tf_op jit(solution)/shard_map/ppermute | solution.py:19
  93.2 0.0 collective-permute-start.12
  93.2 0.0 collective-permute-done.11
  93.3 5.3 %collective-permute-start.13 = (bf16[64,4000]{1,0:T(8,128)(2,1)S(1)}, bf16[64,4000]{1,0:T(8,128)(2,1)S(1)}, u32[]{:S(2)}, u32[]{:S(2)}) collective-permute-start(bf16[64,4000]{1,0:T(8,128)(2,1)S(1)} %collective-permute-done.11), channel_id=1, source_target_pairs={{0,120},{8,0},{16,8},{24,16},{32,24},{40,32},{48,40},{56,48},{64,5... | collective-permute-start | bytes 1536008 | tf_op jit(solution)/shard_map/ppermute | solution.py:26
  98.7 7.3 %collective-permute-done.12 = bf16[64,4000]{1,0:T(8,128)(2,1)S(1)} collective-permute-done((bf16[64,4000]{1,0:T(8,128)(2,1)S(1)}, bf16[64,4000]{1,0:T(8,128)(2,1)S(1)}, u32[]{:S(2)}, u32[]{:S(2)}) %collective-permute-start.12) | collective-permute-done | bytes 512032 | tf_op jit(solution)/shard_map/ppermute | solution.py:19
  106.0 0.0 collective-permute-start.14
  106.0 0.0 collective-permute-done.13
  106.1 12.4 %collective-permute-done.14 = bf16[64,4000]{1,0:T(8,128)(2,1)S(1)} collective-permute-done((bf16[64,4000]{1,0:T(8,128)(2,1)S(1)}, bf16[64,4000]{1,0:T(8,128)(2,1)S(1)}, u32[]{:S(2)}, u32[]{:S(2)}) %collective-permute-start.14) | collective-permute-done | bytes 512032 | tf_op jit(solution)/shard_map/ppermute | solution.py:19
  118.5 4.5 %fusion.31 = (f32[512]{0:T(512)S(1)}, f32[512,4000]{0,1:T(8,128)S(1)}) fusion(bf16[1024,4000]{1,0:T(8,128)(2,1)S(1)} %constant_dynamic-update-slice_fusion, bf16[1024,1024]{1,0:T(8,128)(2,1)S(1)} %fusion.3), kind=kOutput, calls=%fused_computation.70 | convolution fusion | flops 4196351488 | bytes 17631232 | tf_op jit(solution)/shard_map/dot_general | solution.py:44
  123.0 9.2 %fusion.32 = (f32[512]{0:T(512)S(1)}, f32[512,4000]{0,1:T(8,128)}) fusion(bf16[1024,4000]{1,0:T(8,128)(2,1)S(1)} %constant_dynamic-update-slice_fusion, bf16[1024,1024]{1,0:T(8,128)(2,1)S(1)} %fusion.3), kind=kOutput, calls=%fused_computation.71 | convolution fusion | flops 4196351488 | bytes 17631232 | tf_op jit(solution)/shard_map/dot_general | solution.py:44
  132.2 7.8 %exponential_reduce_fusion.1 = (f32[512]{0:T(512)S(1)}, f32[512]{0:T(512)S(1)}, f32[512]{0:T(512)S(1)}, f32[512]{0:T(512)S(1)}, f32[512]{0:T(512)S(1)}, /*index=5*/f32[512]{0:T(512)S(1)}) fusion(f32[512,4000]{0,1:T(8,128)S(1)} %get-tuple-element.32, f32[512]{0:T(512)S(1)} %get-tuple-element.31, s32[512]{0:T(512)S(1)} %bitcast.63, s32[4000]{0:T(1024)S(1)} %iota_add_fusion, ...), kind=kLoop, calls=%fused_computation.3 | loop fusion | flops 28668928 | bytes 16420480 | tf_op jit(solution)/shard_map/reduce_sum | solution.py:48
  140.0 0.7 broadcast_in_dim.17
  140.7 4.3 %all-to-all-start = ((f32[8,4,1024]{2,1,0:T(4,128)}), f32[8,4,1024]{2,1,0:T(4,128)S(1)}, u32[]{:S(2)}, u32[]{:S(2)}) async-start(f32[8,4,1024]{2,1,0:T(4,128)} %broadcast_in_dim.17), calls=%async_computation | async-start | bytes 262144 | tf_op jit(solution)/shard_map/all_to_all | solution.py:60
  145.0 6.1 %all-to-all-done = f32[8,4,1024]{2,1,0:T(4,128)S(1)} async-done(((f32[8,4,1024]{2,1,0:T(4,128)}), f32[8,4,1024]{2,1,0:T(4,128)S(1)}, u32[]{:S(2)}, u32[]{:S(2)}) %all-to-all-start) | async-done | bytes 131104 | tf_op jit(solution)/shard_map/all_to_all | solution.py:60
  151.1 0.1 fusion.29
  151.3 0.8 fusion.27
  152.1 0.2 fusion.13
  152.3 10.1 %all_to_all.10 = f32[16,4,3]{1,2,0:T(4,128)S(1)} all-to-all(f32[16,4,3]{1,2,0:T(4,128)S(1)} %broadcast_in_dim.19), channel_id=1, replica_groups=mesh['dp'=16,'vocab'=8] {'dp'}, dimensions={0} | all-to-all | bytes 1536 | tf_op jit(solution)/shard_map/all_to_all | solution.py:82
  162.5 0.6 pad_maximum_fusion
  (34 shorter events, 0.8 us)
Async XLA Ops:
  0.6 13.1 %copy-start = (bf16[64,4000]{1,0:T(8,128)(2,1)S(1)}, bf16[64,4000]{1,0:T(8,128)(2,1)}, u32[]{:S(2)}) copy-start(bf16[64,4000]{1,0:T(8,128)(2,1)} %param.9) | copy-start | bytes 1536004
  0.6 18.9 %collective-permute-start = (bf16[64,4000]{1,0:T(8,128)(2,1)}, bf16[64,4000]{1,0:T(8,128)(2,1)}, u32[]{:S(2)}, u32[]{:S(2)}) collective-permute-start(bf16[64,4000]{1,0:T(8,128)(2,1)} %param.9), channel_id=1, source_target_pairs={{0,8},{8,16},{16,24},{24,32},{32,40},{40,48},{48,56},{56,64},{64,7... | collective-permute-start | bytes 1536008 | tf_op jit(solution)/shard_map/ppermute | solution.py:19
  2.4 17.2 %collective-permute-start.1 = (bf16[64,4000]{1,0:T(8,128)(2,1)}, bf16[64,4000]{1,0:T(8,128)(2,1)S(1)}, u32[]{:S(2)}, u32[]{:S(2)}) collective-permute-start(bf16[64,4000]{1,0:T(8,128)(2,1)} %param.9), channel_id=1, source_target_pairs={{0,120},{8,0},{16,8},{24,16},{32,24},{40,32},{48,40},{56,48},{64,5... | collective-permute-start | bytes 1536008 | tf_op jit(solution)/shard_map/ppermute | solution.py:26
  19.5 16.6 %collective-permute-start.2 = (bf16[64,4000]{1,0:T(8,128)(2,1)}, bf16[64,4000]{1,0:T(8,128)(2,1)S(1)}, u32[]{:S(2)}, u32[]{:S(2)}) collective-permute-start(bf16[64,4000]{1,0:T(8,128)(2,1)} %collective-permute-done), channel_id=1, source_target_pairs={{0,8},{8,16},{16,24},{24,32},{32,40},{40,48},{48,56},{56,64},{64,7... | collective-permute-start | bytes 1536008 | tf_op jit(solution)/shard_map/ppermute | solution.py:19
  19.6 16.6 %collective-permute-start.3 = (bf16[64,4000]{1,0:T(8,128)(2,1)S(1)}, bf16[64,4000]{1,0:T(8,128)(2,1)S(1)}, u32[]{:S(2)}, u32[]{:S(2)}) collective-permute-start(bf16[64,4000]{1,0:T(8,128)(2,1)S(1)} %collective-permute-done.1), channel_id=1, source_target_pairs={{0,120},{8,0},{16,8},{24,16},{32,24},{40,32},{48,40},{56,48},{64,5... | collective-permute-start | bytes 1536008 | tf_op jit(solution)/shard_map/ppermute | solution.py:26
  36.2 15.6 %collective-permute-start.4 = (bf16[64,4000]{1,0:T(8,128)(2,1)S(1)}, bf16[64,4000]{1,0:T(8,128)(2,1)S(1)}, u32[]{:S(2)}, u32[]{:S(2)}) collective-permute-start(bf16[64,4000]{1,0:T(8,128)(2,1)S(1)} %collective-permute-done.2), channel_id=1, source_target_pairs={{0,8},{8,16},{16,24},{24,32},{32,40},{40,48},{48,56},{56,64},{64,7... | collective-permute-start | bytes 1536008 | tf_op jit(solution)/shard_map/ppermute | solution.py:19
  36.2 15.6 %collective-permute-start.5 = (bf16[64,4000]{1,0:T(8,128)(2,1)S(1)}, bf16[64,4000]{1,0:T(8,128)(2,1)S(1)}, u32[]{:S(2)}, u32[]{:S(2)}) collective-permute-start(bf16[64,4000]{1,0:T(8,128)(2,1)S(1)} %collective-permute-done.3), channel_id=1, source_target_pairs={{0,120},{8,0},{16,8},{24,16},{32,24},{40,32},{48,40},{56,48},{64,5... | collective-permute-start | bytes 1536008 | tf_op jit(solution)/shard_map/ppermute | solution.py:26
  51.7 14.7 %collective-permute-start.6 = (bf16[64,4000]{1,0:T(8,128)(2,1)S(1)}, bf16[64,4000]{1,0:T(8,128)(2,1)S(1)}, u32[]{:S(2)}, u32[]{:S(2)}) collective-permute-start(bf16[64,4000]{1,0:T(8,128)(2,1)S(1)} %collective-permute-done.4), channel_id=1, source_target_pairs={{0,8},{8,16},{16,24},{24,32},{32,40},{40,48},{48,56},{56,64},{64,7... | collective-permute-start | bytes 1536008 | tf_op jit(solution)/shard_map/ppermute | solution.py:19
  51.7 14.7 %collective-permute-start.7 = (bf16[64,4000]{1,0:T(8,128)(2,1)S(1)}, bf16[64,4000]{1,0:T(8,128)(2,1)S(1)}, u32[]{:S(2)}, u32[]{:S(2)}) collective-permute-start(bf16[64,4000]{1,0:T(8,128)(2,1)S(1)} %collective-permute-done.5), channel_id=1, source_target_pairs={{0,120},{8,0},{16,8},{24,16},{32,24},{40,32},{48,40},{56,48},{64,5... | collective-permute-start | bytes 1536008 | tf_op jit(solution)/shard_map/ppermute | solution.py:26
  66.4 13.8 %collective-permute-start.8 = (bf16[64,4000]{1,0:T(8,128)(2,1)S(1)}, bf16[64,4000]{1,0:T(8,128)(2,1)S(1)}, u32[]{:S(2)}, u32[]{:S(2)}) collective-permute-start(bf16[64,4000]{1,0:T(8,128)(2,1)S(1)} %collective-permute-done.6), channel_id=1, source_target_pairs={{0,8},{8,16},{16,24},{24,32},{32,40},{40,48},{48,56},{56,64},{64,7... | collective-permute-start | bytes 1536008 | tf_op jit(solution)/shard_map/ppermute | solution.py:19
  66.4 13.8 %collective-permute-start.9 = (bf16[64,4000]{1,0:T(8,128)(2,1)S(1)}, bf16[64,4000]{1,0:T(8,128)(2,1)S(1)}, u32[]{:S(2)}, u32[]{:S(2)}) collective-permute-start(bf16[64,4000]{1,0:T(8,128)(2,1)S(1)} %collective-permute-done.7), channel_id=1, source_target_pairs={{0,120},{8,0},{16,8},{24,16},{32,24},{40,32},{48,40},{56,48},{64,5... | collective-permute-start | bytes 1536008 | tf_op jit(solution)/shard_map/ppermute | solution.py:26
  80.3 13.0 %collective-permute-start.10 = (bf16[64,4000]{1,0:T(8,128)(2,1)S(1)}, bf16[64,4000]{1,0:T(8,128)(2,1)S(1)}, u32[]{:S(2)}, u32[]{:S(2)}) collective-permute-start(bf16[64,4000]{1,0:T(8,128)(2,1)S(1)} %collective-permute-done.8), channel_id=1, source_target_pairs={{0,8},{8,16},{16,24},{24,32},{32,40},{40,48},{48,56},{56,64},{64,7... | collective-permute-start | bytes 1536008 | tf_op jit(solution)/shard_map/ppermute | solution.py:19
  80.3 13.0 %collective-permute-start.11 = (bf16[64,4000]{1,0:T(8,128)(2,1)S(1)}, bf16[64,4000]{1,0:T(8,128)(2,1)S(1)}, u32[]{:S(2)}, u32[]{:S(2)}) collective-permute-start(bf16[64,4000]{1,0:T(8,128)(2,1)S(1)} %collective-permute-done.9), channel_id=1, source_target_pairs={{0,120},{8,0},{16,8},{24,16},{32,24},{40,32},{48,40},{56,48},{64,5... | collective-permute-start | bytes 1536008 | tf_op jit(solution)/shard_map/ppermute | solution.py:26
  93.2 12.8 %collective-permute-start.12 = (bf16[64,4000]{1,0:T(8,128)(2,1)S(1)}, bf16[64,4000]{1,0:T(8,128)(2,1)S(1)}, u32[]{:S(2)}, u32[]{:S(2)}) collective-permute-start(bf16[64,4000]{1,0:T(8,128)(2,1)S(1)} %collective-permute-done.10), channel_id=1, source_target_pairs={{0,8},{8,16},{16,24},{24,32},{32,40},{40,48},{48,56},{56,64},{64,7... | collective-permute-start | bytes 1536008 | tf_op jit(solution)/shard_map/ppermute | solution.py:19
  93.3 12.8 %collective-permute-start.13 = (bf16[64,4000]{1,0:T(8,128)(2,1)S(1)}, bf16[64,4000]{1,0:T(8,128)(2,1)S(1)}, u32[]{:S(2)}, u32[]{:S(2)}) collective-permute-start(bf16[64,4000]{1,0:T(8,128)(2,1)S(1)} %collective-permute-done.11), channel_id=1, source_target_pairs={{0,120},{8,0},{16,8},{24,16},{32,24},{40,32},{48,40},{56,48},{64,5... | collective-permute-start | bytes 1536008 | tf_op jit(solution)/shard_map/ppermute | solution.py:26
  106.0 12.5 %collective-permute-start.14 = (bf16[64,4000]{1,0:T(8,128)(2,1)S(1)}, bf16[64,4000]{1,0:T(8,128)(2,1)S(1)}, u32[]{:S(2)}, u32[]{:S(2)}) collective-permute-start(bf16[64,4000]{1,0:T(8,128)(2,1)S(1)} %collective-permute-done.12), channel_id=1, source_target_pairs={{0,8},{8,16},{16,24},{24,32},{32,40},{40,48},{48,56},{56,64},{64,7... | collective-permute-start | bytes 1536008 | tf_op jit(solution)/shard_map/ppermute | solution.py:19
  132.2 12.8 %copy-start.1 = (s32[2]{0:T(128)S(1)}, s32[2]{0:T(128)}, u32[]{:S(2)}) copy-start(s32[2]{0:T(128)} %param.11) | copy-start | bytes 28
  132.2 19.9 %copy-start.3 = (s32[2,1]{0,1:T(1,128)S(1)}, s32[2,1]{0,1:T(1,128)}, u32[]{:S(2)}) copy-start(s32[2,1]{0,1:T(1,128)} %param.12) | copy-start | bytes 28
  132.2 30.3 %copy-start.2 = (f32[4]{0:T(128)S(1)}, f32[4]{0:T(128)}, u32[]{:S(2)}) copy-start(f32[4]{0:T(128)} %param.13) | copy-start | bytes 52
  140.7 10.4 %all-to-all-start = ((f32[8,4,1024]{2,1,0:T(4,128)}), f32[8,4,1024]{2,1,0:T(4,128)S(1)}, u32[]{:S(2)}, u32[]{:S(2)}) async-start(f32[8,4,1024]{2,1,0:T(4,128)} %broadcast_in_dim.17), calls=%async_computation | async-start | bytes 262144 | tf_op jit(solution)/shard_map/all_to_all | solution.py:60
